TPU v7x, 256 devices: a whole 4x4x8 slice. The times are simulated.
256 devices in a mesh: expert: 16 (over z, core), tensor: 16 (over y, x).
Axes of the slice: x: 4, y: 4, z: 8, core: 2. Of those that a mesh axis runs over, the one named last changes fastest.
Arguments:
- residual_in: bfloat16 [22528, 1024], P(('expert', 'tensor')), may hold values from -6 to 6
- attn_heads: bfloat16 [1024, 22528], P('tensor', 'expert'), may hold values from -6 to 6
- out_proj: bfloat16 [1024, 1024], P('tensor'), may hold values from -0.1875 to 0.1875
- gain_first: float32 [1024], replicated, may hold values from 0.25 to 1.75
- router_weight: float32 [1024, 16], replicated, may hold values from -0.046875 to 0.046875
- routes: int32 [22528, 2], P(('expert', 'tensor')), may hold values from 0 to 15, all different within a row; in each aligned block of 88 rows (0 to 87, 88 to 175, ...) at most 22 rows name the same one
- w_gate: bfloat16 [16, 2816, 1024], P('expert', 'tensor'), may hold values from -0.1875 to 0.1875
- w_upward: bfloat16 [16, 2816, 1024], P('expert', 'tensor'), may hold values from -0.1875 to 0.1875
- w_downward: bfloat16 [16, 2816, 1024], P('expert', 'tensor'), may hold values from -0.21875 to 0.21875
- gain_second: float32 [1024], replicated, may hold values from 0.25 to 1.75
Outputs:
- residual_out: bfloat16 [22528, 1024], P(('expert', 'tensor'))
- next_normed: bfloat16 [22528, 1024], P(('expert', 'tensor'))
Inputs may be any that keep to these rules, and one draw needn't show every extreme that they name: `routes`: each row names two different experts; among the rows of one device no expert is named more than 22 times, and some expert reaches 22.
All inputs are finite; a program needn't handle non-finite values.
Results may differ from a plain program's by a relative error of at most 0.012.
Values may be sent and summed in bfloat16 or wider, within the bound.
No kernel may reach another device: no remote copies, remote signals or barrier semaphores. Data moves between devices by JAX's collectives and lax.ppermute only.
A program may use at most 128 MiB of HBM per device.

v0:
```python
import jax
import jax.numpy as jnp
from jax import lax
from jax.sharding import PartitionSpec as P


def rms_scale(values, gain):
    wide = values.astype(jnp.float32)
    scale = lax.rsqrt(jnp.mean(wide * wide, axis=-1, keepdims=True) + 1e-06)
    return (wide * scale * gain).astype(jnp.bfloat16)


def expert_block(inputs, gate_rows, up_rows, down_rows):
    gate_part = lax.dot_general(
        inputs, gate_rows, (((1,), (1,)), ((), ())), preferred_element_type=jnp.float32
    )
    up_part = lax.dot_general(
        inputs, up_rows, (((1,), (1,)), ((), ())), preferred_element_type=jnp.float32
    )
    hid = (jax.nn.gelu(gate_part, approximate=True) * up_part).astype(jnp.bfloat16)
    return jnp.dot(hid, down_rows, preferred_element_type=jnp.float32)


def per_device(
    residual_in,
    attn_heads,
    out_proj,
    gain_first,
    router_weight,
    routes,
    w_gate,
    w_upward,
    w_downward,
    gain_second,
):
    row_count = residual_in.shape[0]
    width = residual_in.shape[1]
    n_expert = lax.axis_size("expert")
    capacity = 4 * row_count // n_expert
    block = attn_heads
    projected = lax.psum_scatter(
        lax.dot_general(
            block, out_proj, (((0,), (0,)), ((), ())), preferred_element_type=jnp.float32
        ),
        "tensor",
        scatter_dimension=0,
        tiled=True,
    )
    hidden_one = (residual_in.astype(jnp.float32) + projected).astype(jnp.bfloat16)
    normed = rms_scale(hidden_one, gain_first)
    logits = jnp.dot(normed.astype(jnp.float32), router_weight, precision=lax.Precision.HIGHEST)
    router_probs = jax.nn.softmax(logits, axis=-1)
    picked = jnp.take_along_axis(router_probs, routes, axis=1)
    gate_weights = picked / jnp.sum(picked, axis=1, keepdims=True)
    flat_ids = routes.reshape(-1)
    expert_iota = jnp.arange(n_expert, dtype=jnp.int32)
    onehot = (flat_ids[:, None] == expert_iota[None, :]).astype(jnp.int32)
    earlier = jnp.cumsum(onehot, axis=0) - onehot
    slot_index = jnp.sum(earlier * onehot, axis=1)
    target = flat_ids * capacity + slot_index
    slot_iota = jnp.arange(n_expert * capacity, dtype=jnp.int32)
    placing = (slot_iota[:, None] == target[None, :]).astype(jnp.bfloat16)
    repeated = jnp.repeat(normed, 2, axis=0)
    send_slots = jnp.dot(placing, repeated, preferred_element_type=jnp.float32).astype(jnp.bfloat16)
    send_slots = send_slots.reshape(n_expert, capacity, width)
    received = lax.all_to_all(send_slots, "expert", split_axis=0, concat_axis=0, tiled=True)
    slot_total = n_expert * capacity
    rows_in = received.reshape(slot_total, width)
    gate_rows = w_gate[0]
    up_rows = w_upward[0]
    down_rows = w_downward[0]
    all_rows = lax.all_gather(rows_in, "tensor", axis=0, tiled=True)
    block = all_rows
    expert_sum = lax.psum_scatter(
        expert_block(block, gate_rows, up_rows, down_rows).astype(jnp.bfloat16),
        "tensor",
        scatter_dimension=0,
        tiled=True,
    )
    expert_out = expert_sum.reshape(n_expert, capacity, width)
    returned = lax.all_to_all(expert_out, "expert", split_axis=0, concat_axis=0, tiled=True)
    returned = returned.reshape(slot_total, width)
    per_route = lax.dot_general(
        placing, returned, (((0,), (0,)), ((), ())), preferred_element_type=jnp.float32
    )
    per_route = per_route.reshape(row_count, 2, width)
    mixed = jnp.sum(gate_weights[:, :, None] * per_route, axis=1)
    residual_out = (hidden_one.astype(jnp.float32) + mixed).astype(jnp.bfloat16)
    next_normed = rms_scale(residual_out, gain_second)
    return (residual_out, next_normed)


def solution(mesh):
    placed = (
        P(("expert", "tensor"), None),
        P("tensor", "expert"),
        P("tensor", None),
        P(),
        P(),
        P(("expert", "tensor"), None),
        P("expert", "tensor", None),
        P("expert", "tensor", None),
        P("expert", "tensor", None),
        P(),
    )
    return jax.shard_map(
        per_device,
        mesh=mesh,
        in_specs=placed,
        out_specs=(P(("expert", "tensor"), None), P(("expert", "tensor"), None)),
        check_vma=False,
    )
```

profile of v0, /device:TPU:1, one launch (start us, length us, event | category | flops | bytes accessed | tf_op | source)
XLA Modules:
  0.0 380.7 jit_solution(14872669456772548435)
XLA Ops:
  7.2 0.0 copy-start
  7.2 0.0 reduce-scatter.7.cloned.1.call-start
  7.2 4.4 %fusion.38 = f32[1408,1024]{1,0:T(8,128)} fusion(bf16[64,1408]{1,0:T(8,128)(2,1)} %param.11, bf16[64,1024]{1,0:T(8,128)(2,1)} %param.12), kind=kOutput, calls=%fused_computation.66 | convolution fusion | flops 184549376 | bytes 6078464 | tf_op jit(solution)/shard_map/dot_general | solution.py:42
  11.7 0.0 reduce-scatter.7.cloned.1.call-update
  11.7 0.0 all-gather.2.cloned.1.call-start
  11.7 0.6 copy-done.5
  12.3 0.1 copy.34
  12.4 0.1 reshape.109
  12.6 0.6 reduce-window.6
  13.2 0.2 slice_reduce_fusion
  13.4 0.1 bitcast_bitcast_fusion
  13.5 86.2 %reduce-scatter.7.cloned.1.call-done = f32[88,1024]{1,0:T(8,128)} async-done(((f32[1408,1024]{1,0:T(8,128)}), f32[88,1024]{1,0:T(8,128)}) %reduce-scatter.7.cloned.1.call-update) | async-done | bytes 360464
  99.7 0.0 copy-done.3
  99.7 1.1 fusion.16
  100.9 0.0 copy-done.6
  100.9 0.0 copy-start.2
  100.9 0.1 fusion.18
  101.0 0.2 broadcast_in_dim.7
  101.2 0.1 reshape.112
  101.4 0.3 convolution_convert_fusion.1
  101.7 0.2 reshape.113
  101.9 32.1 %all_to_all.10 = bf16[16,22,1024]{2,1,0:T(8,128)(2,1)S(1)} all-to-all(bf16[16,22,1024]{2,1,0:T(8,128)(2,1)S(1)} %reshape.113), channel_id=1, replica_groups=mesh['expert'=16,'tensor'=16] {'expert'}, dimensions={0} | all-to-all | bytes 1441792 | tf_op jit(solution)/shard_map/all_to_all | solution.py:66
  134.1 1.1 reshape.114
  135.1 0.0 all-gather.2.cloned.1.call-update
  135.1 0.0 copy-start.8
  135.2 0.0 reduce-scatter.5.cloned.1.call-start
  135.2 84.5 %all-gather.2.cloned.1.call-done = bf16[5632,1024]{1,0:T(8,128)(2,1)} async-done(((bf16[352,1024]{1,0:T(8,128)(2,1)}), bf16[5632,1024]{1,0:T(8,128)(2,1)}) %all-gather.2.cloned.1.call-update) | async-done | bytes 11534352 | tf_op jit(solution)/shard_map/all_gather | solution.py:72
  219.7 0.0 copy-done.2
  219.7 10.2 %fusion.23 = f32[5632,176]{0,1:T(8,128)} fusion(bf16[5632,1024]{1,0:T(8,128)(2,1)} %all-gather.2.cloned.1.call-done, bf16[1,176,1024]{2,1,0:T(8,128)(2,1)S(1)} %copy-done.2), kind=kOutput, calls=%fused_computation.33 | convolution fusion | flops 2030043136 | bytes 15859712 | tf_op jit(solution)/shard_map/dot_general | solution.py:14
  229.9 13.1 %convolution_convert_fusion = bf16[5632,1024]{1,0:T(8,128)(2,1)} fusion(bf16[5632,1024]{1,0:T(8,128)(2,1)} %all-gather.2.cloned.1.call-done, f32[5632,176]{0,1:T(8,128)} %fusion.23, bf16[1,176,1024]{2,1,0:T(8,128)(2,1)S(1)} %copy-done, bf16[1,176,1024]{2,1,0:T(8,128)(2,1)S(1)} %copy-done.8), kind=kOutput, calls=%fused_computation.1 | convolution fusion | flops 4075765760 | bytes 27754496 | tf_op jit(solution)/shard_map/dot_general | solution.py:21
  243.0 0.0 reduce-scatter.5.cloned.1.call-update
  243.0 96.4 %reduce-scatter.5.cloned.1.call-done = bf16[352,1024]{1,0:T(8,128)(2,1)} async-done(((bf16[5632,1024]{1,0:T(8,128)(2,1)}), bf16[352,1024]{1,0:T(8,128)(2,1)}) %reduce-scatter.5.cloned.1.call-update) | async-done | bytes 720912 | tf_op jit(solution)/shard_map/reduce_scatter | solution.py:74
  339.5 2.1 reshape.115
  341.6 8.3 %all-to-all-start.1 = ((bf16[16,22,1024]{2,1,0:T(8,128)(2,1)}), bf16[16,22,1024]{2,1,0:T(8,128)(2,1)S(1)}, u32[]{:S(2)}, u32[]{:S(2)}) async-start(bf16[16,22,1024]{2,1,0:T(8,128)(2,1)} %reshape.115), calls=%async_computation.2 | async-start | bytes 1572864 | tf_op jit(solution)/shard_map/all_to_all | solution.py:81
  349.9 0.1 copy.32
  350.0 0.1 reshape.118
  350.1 0.1 iota_compare_fusion.2
  350.3 0.1 eq.57
  350.4 0.3 fusion.37
  350.7 0.0 copy-start.7
  350.7 2.3 gather_fusion
  353.0 0.1 reshape.121
  353.1 0.1 copy.33
  353.2 19.4 %all-to-all-done.1 = bf16[16,22,1024]{2,1,0:T(8,128)(2,1)S(1)} async-done(((bf16[16,22,1024]{2,1,0:T(8,128)(2,1)}), bf16[16,22,1024]{2,1,0:T(8,128)(2,1)S(1)}, u32[]{:S(2)}, u32[]{:S(2)}) %all-to-all-start.1) | async-done | bytes 720928 | tf_op jit(solution)/shard_map/all_to_all | solution.py:81
  372.6 0.2 reshape.129
  372.8 0.4 fusion.12
  373.2 0.2 fusion.13
  373.4 0.8 fusion.15
  (23 shorter events, 0.2 us)
Async XLA Ops:
  7.2 222.7 %copy-start = (bf16[1,176,1024]{2,1,0:T(8,128)(2,1)S(1)}, bf16[1,176,1024]{2,1,0:T(8,128)(2,1)}, u32[]{:S(2)}) copy-start(bf16[1,176,1024]{2,1,0:T(8,128)(2,1)} %param.18) | copy-start | bytes 1081348
  7.2 92.5 %reduce-scatter.7.cloned.1.call-start = ((), (), s32[]{:S(2)}) async-start(), calls=%async_computation.6 | async-start | bytes 6127616
  11.7 0.7 copy-start.5
  11.7 88.1 %copy-start.3 = (bf16[88,1024]{1,0:T(8,128)(2,1)S(1)}, bf16[88,1024]{1,0:T(8,128)(2,1)}, u32[]{:S(2)}) copy-start(bf16[88,1024]{1,0:T(8,128)(2,1)} %param.10) | copy-start | bytes 540676
  11.7 89.2 %copy-start.6 = (f32[1024]{0:T(1024)S(1)}, f32[1024]{0:T(1024)}, u32[]{:S(2)}) copy-start(f32[1024]{0:T(1024)} %param.13) | copy-start | bytes 12292
  11.7 208.0 %all-gather.2.cloned.1.call-start = ((), (), s32[]{:S(2)}) async-start(), calls=%async_computation.4 | async-start | bytes 12255232 | tf_op jit(solution)/shard_map/all_gather | solution.py:72
  100.9 118.8 %copy-start.2 = (bf16[1,176,1024]{2,1,0:T(8,128)(2,1)S(1)}, bf16[1,176,1024]{2,1,0:T(8,128)(2,1)}, u32[]{:S(2)}) copy-start(bf16[1,176,1024]{2,1,0:T(8,128)(2,1)} %param.16) | copy-start | bytes 1081348
  135.1 94.8 %copy-start.8 = (bf16[1,176,1024]{2,1,0:T(8,128)(2,1)S(1)}, bf16[1,176,1024]{2,1,0:T(8,128)(2,1)}, u32[]{:S(2)}) copy-start(bf16[1,176,1024]{2,1,0:T(8,128)(2,1)} %param.17) | copy-start | bytes 1081348
  135.2 204.3 %reduce-scatter.5.cloned.1.call-start = ((), (), s32[]{:S(2)}) async-start(), calls=%async_computation.5 | async-start | bytes 12255232 | tf_op jit(solution)/shard_map/reduce_scatter | solution.py:74
  243.0 107.4 %copy-start.4 = (f32[1024,16]{0,1:T(8,128)S(1)}, f32[1024,16]{0,1:T(8,128)}, u32[]{:S(2)}) copy-start(f32[1024,16]{0,1:T(8,128)} %param.14) | copy-start | bytes 196612
  341.6 31.1 %all-to-all-start.1 = ((bf16[16,22,1024]{2,1,0:T(8,128)(2,1)}), bf16[16,22,1024]{2,1,0:T(8,128)(2,1)S(1)}, u32[]{:S(2)}, u32[]{:S(2)}) async-start(bf16[16,22,1024]{2,1,0:T(8,128)(2,1)} %reshape.115), calls=%async_computation.2 | async-start | bytes 1572864 | tf_op jit(solution)/shard_map/all_to_all | solution.py:81
  350.7 22.7 %copy-start.7 = (f32[1024]{0:T(1024)S(1)}, f32[1024]{0:T(1024)}, u32[]{:S(2)}) copy-start(f32[1024]{0:T(1024)} %param.19) | copy-start | bytes 12292
  373.3 0.8 copy-start.1
Sparse Core Ops, SparseCore 0:
  11.8 87.8 reduce-scatter.6
  135.3 84.3 all-gather.1
  243.2 96.2 reduce-scatter.4
where the time goes:
time: 381 us
  waiting for transfers between devices  287 us (75%)
  blocking collectives  32.1 us (8%)
  matrix products  28.7 us (8%)
  between operations  14 us (4%)
  starting transfers between devices  8.46 us (2%)
  local copies, waits for them, and re-layouts  7.73 us (2%)
    reduce_scatter x1, waiting for transfers between devices, per_device(): lax.psum_scatter(expert_block(block, gate_rows, up_rows, down_rows).astyp...  96.4 us
    unnamed x4, waiting for transfers between devices  86.2 us
    all_gather x1, waiting for transfers between devices, per_device(): all_rows = lax.all_gather(rows_in, 'tensor', axis=0, tiled=True)  84.5 us
    all_to_all x1, blocking collectives, per_device(): lax.all_to_all(send_slots, 'expert', split_axis=0, concat_axis=0, tiled=T...  32.1 us
    all_to_all x1, waiting for transfers between devices, per_device(): lax.all_to_all(expert_out, 'expert', split_axis=0, concat_axis=0, tiled=T...  19.4 us
    dot_general x1, matrix products, expert_block(): return jnp.dot(hid, down_rows, preferred_element_type=jnp.float32)  13.1 us
    dot_general x1, matrix products, expert_block(): lax.dot_general(inputs, gate_rows, (((1,), (1,)), ((), ())), preferred_el...  10.2 us
    all_to_all x1, starting transfers between devices, per_device(): lax.all_to_all(expert_out, 'expert', split_axis=0, concat_axis=0, tiled=T...  8.33 us
  transfers between devices with their start and end apart: 4, of which 4 were waited for; matrix products, arithmetic and copies ran while one was open for 1% of the time, Pallas kernels for 0%

commit v1 on v0

--- a/solution.py
+++ b/solution.py
@@ -1,7 +1,17 @@
+import functools
 import jax
 import jax.numpy as jnp
 from jax import lax
 from jax.sharding import PartitionSpec as P
+
+
+def part_the_digits(block_here, device_axis):
+    part_next = jnp.stack([block_here for _ in range(lax.axis_size(device_axis))])
+    z2 = lax.all_to_all(part_next, axis_name=device_axis, split_axis=0, concat_axis=0)
+    return jnp.concatenate(z2, axis=0)
+
+
+_handle_stops_all = functools.partial(part_the_digits, device_axis="tensor")
 
 
 def rms_scale(values, gain):
@@ -69,7 +79,7 @@
     gate_rows = w_gate[0]
     up_rows = w_upward[0]
     down_rows = w_downward[0]
-    all_rows = lax.all_gather(rows_in, "tensor", axis=0, tiled=True)
+    all_rows = _handle_stops_all(rows_in)
     block = all_rows
     expert_sum = lax.psum_scatter(
         expert_block(block, gate_rows, up_rows, down_rows).astype(jnp.bfloat16),

time: 381 us -> 433 us (1.14)
  blocking collectives: 32.1 us -> 167 us
  waiting for transfers between devices: 287 us -> 198 us
  local copies, waits for them, and re-layouts: 7.73 us -> 16.9 us
    all_to_all x0 -> x1, blocking collectives: none -> 135 us  [part_the_digits(): lax.all_to_all(part_next, axis_name=device_axis, split_axis=0, concat_axi...]
    all_gather x1 -> x0, waiting for transfers between devices: 84.5 us -> none  [per_device(): all_rows = lax.all_gather(rows_in, 'tensor', axis=0, tiled=True)]
    another operation x1 -> x3, local copies, waits for them, and re-layouts: 0.01 us -> 6.04 us  [the longest x2 6.03 us: part_the_digits(): jnp.stack([block_here for _ in range(lax.axis_size(device_axis))])]
    unnamed x4 -> x3, waiting for transfers between devices: 86.2 us -> 86.2 us
  transfers between devices with their start and end apart: 4 -> 3, of which waited for: 4 -> 3; matrix products, arithmetic and copies ran while one was open for 1% -> 1% of each run, Pallas kernels for 0% -> 0%
where the time goes in v1:
time: 433 us
  waiting for transfers between devices  198 us (46%)
  blocking collectives  167 us (39%)
  matrix products  24.5 us (6%)
  local copies, waits for them, and re-layouts  16.9 us (4%)
  between operations  14.2 us (3%)
  starting transfers between devices  8.41 us (2%)
    all_to_all x1, blocking collectives, part_the_digits(): lax.all_to_all(part_next, axis_name=device_axis, split_axis=0, concat_axi...  135 us
    reduce_scatter x1, waiting for transfers between devices, per_device(): lax.psum_scatter(expert_block(block, gate_rows, up_rows, down_rows).astyp...  92.6 us
    unnamed x3, waiting for transfers between devices  86.2 us
    all_to_all x1, blocking collectives, per_device(): lax.all_to_all(send_slots, 'expert', split_axis=0, concat_axis=0, tiled=T...  32.1 us
    all_to_all x1, waiting for transfers between devices, per_device(): lax.all_to_all(expert_out, 'expert', split_axis=0, concat_axis=0, tiled=T...  19.4 us
    dot_general x1, matrix products, expert_block(): return jnp.dot(hid, down_rows, preferred_element_type=jnp.float32)  13.2 us
  transfers between devices with their start and end apart: 3, of which 3 were waited for; matrix products, arithmetic and copies ran while one was open for 1% of the time, Pallas kernels for 0%

profile of v1, /device:TPU:1, one launch (start us, length us, event | category | flops | bytes accessed | tf_op | source)
XLA Modules:
  0.0 432.6 jit_solution(5425296063510411442)
XLA Ops:
  7.2 0.0 copy-start
  7.2 0.0 reduce-scatter.7.cloned.1.call-start
  7.2 4.4 %fusion.38 = f32[1408,1024]{1,0:T(8,128)} fusion(bf16[64,1408]{1,0:T(8,128)(2,1)} %param.11, bf16[64,1024]{1,0:T(8,128)(2,1)} %param.12), kind=kOutput, calls=%fused_computation.66 | convolution fusion | flops 184549376 | bytes 6078464 | tf_op jit(solution)/shard_map/dot_general | solution.py:52
  11.7 0.0 reduce-scatter.7.cloned.1.call-update
  11.7 0.0 reduce-scatter.5.cloned.1.call-start
  11.7 0.6 copy-done.6
  12.3 0.1 copy.34
  12.4 0.1 reshape.111
  12.6 0.6 reduce-window.6
  13.2 0.2 slice_reduce_fusion
  13.4 0.1 bitcast_bitcast_fusion
  13.5 86.2 %reduce-scatter.7.cloned.1.call-done = f32[88,1024]{1,0:T(8,128)} async-done(((f32[1408,1024]{1,0:T(8,128)}), f32[88,1024]{1,0:T(8,128)}) %reduce-scatter.7.cloned.1.call-update) | async-done | bytes 360464
  99.7 0.0 copy-done.4
  99.7 1.1 fusion.16
  100.9 0.0 copy-done.7
  100.9 0.1 fusion.18
  101.0 0.2 broadcast_in_dim.7
  101.2 0.1 reshape.114
  101.3 0.3 convolution_convert_fusion.1
  101.7 0.2 reshape.115
  101.9 32.1 %all_to_all.15 = bf16[16,22,1024]{2,1,0:T(8,128)(2,1)S(1)} all-to-all(bf16[16,22,1024]{2,1,0:T(8,128)(2,1)S(1)} %reshape.115), channel_id=1, replica_groups=mesh['expert'=16,'tensor'=16] {'expert'}, dimensions={0} | all-to-all | bytes 1441792 | tf_op jit(solution)/shard_map/all_to_all | solution.py:76
  134.0 0.2 stack_reshape.2
  134.2 5.8 %stack.3 = bf16[16,352,1024]{2,1,0:T(8,128)(2,1)} broadcast(bf16[352,1024]{1,0:T(8,128)(2,1)S(1)} %stack_reshape.2), dimensions={1,2} | broadcast | bytes 12255232 | tf_op jit(solution)/shard_map/stack | solution.py:9
  140.1 135.1 %all_to_all.16 = bf16[16,352,1024]{2,1,0:T(8,128)(2,1)S(1)} all-to-all(bf16[16,352,1024]{2,1,0:T(8,128)(2,1)} %stack.3), channel_id=1, replica_groups=mesh['expert'=16,'tensor'=16] {'tensor'}, dimensions={0} | all-to-all | bytes 23068672 | tf_op jit(solution)/shard_map/all_to_all | solution.py:10
  275.2 4.2 copy-done.1
  279.4 0.0 copy-done.3
  279.4 5.9 %fusion.23 = f32[5632,176]{0,1:T(8,128)} fusion(bf16[5632,1024]{1,0:T(8,128)(2,1)S(1)} %bitcast.36, bf16[1,176,1024]{2,1,0:T(8,128)(2,1)S(1)} %copy-done.3), kind=kOutput, calls=%fused_computation.33 | convolution fusion | flops 2030043136 | bytes 15859712 | tf_op jit(solution)/shard_map/dot_general | solution.py:24
  285.4 0.0 copy-done
  285.4 13.2 %convolution_convert_fusion = bf16[5632,1024]{1,0:T(8,128)(2,1)} fusion(bf16[5632,1024]{1,0:T(8,128)(2,1)} %bitcast.37, f32[5632,176]{0,1:T(8,128)} %fusion.23, bf16[1,176,1024]{2,1,0:T(8,128)(2,1)S(1)} %copy-done, bf16[1,176,1024]{2,1,0:T(8,128)(2,1)S(1)} %copy-done.9), kind=kOutput, calls=%fused_computation.1 | convolution fusion | flops 4075765760 | bytes 27754496 | tf_op jit(solution)/shard_map/dot_general | solution.py:31
  298.5 0.0 reduce-scatter.5.cloned.1.call-update
  298.5 92.6 %reduce-scatter.5.cloned.1.call-done = bf16[352,1024]{1,0:T(8,128)(2,1)} async-done(((bf16[5632,1024]{1,0:T(8,128)(2,1)}), bf16[352,1024]{1,0:T(8,128)(2,1)}) %reduce-scatter.5.cloned.1.call-update) | async-done | bytes 720912 | tf_op jit(solution)/shard_map/reduce_scatter | solution.py:84
  391.1 2.1 reshape.117
  393.2 8.3 %all-to-all-start.2 = ((bf16[16,22,1024]{2,1,0:T(8,128)(2,1)}), bf16[16,22,1024]{2,1,0:T(8,128)(2,1)S(1)}, u32[]{:S(2)}, u32[]{:S(2)}) async-start(bf16[16,22,1024]{2,1,0:T(8,128)(2,1)} %reshape.117), calls=%async_computation.3 | async-start | bytes 1572864 | tf_op jit(solution)/shard_map/all_to_all | solution.py:91
  401.5 0.1 copy.32
  401.6 0.1 reshape.120
  401.8 0.1 iota_compare_fusion.2
  401.9 0.1 eq.57
  402.0 0.3 fusion.37
  402.3 0.0 copy-start.8
  402.3 2.3 gather_fusion
  404.6 0.1 reshape.123
  404.7 0.1 copy.33
  404.8 19.4 %all-to-all-done.2 = bf16[16,22,1024]{2,1,0:T(8,128)(2,1)S(1)} async-done(((bf16[16,22,1024]{2,1,0:T(8,128)(2,1)}), bf16[16,22,1024]{2,1,0:T(8,128)(2,1)S(1)}, u32[]{:S(2)}, u32[]{:S(2)}) %all-to-all-start.2) | async-done | bytes 720928 | tf_op jit(solution)/shard_map/all_to_all | solution.py:91
  424.2 0.2 reshape.131
  424.4 0.4 fusion.12
  424.8 0.2 fusion.13
  425.0 0.8 fusion.15
  425.8 0.0 copy-done.2
  (24 shorter events, 0.2 us)
Async XLA Ops:
  7.2 278.2 %copy-start = (bf16[1,176,1024]{2,1,0:T(8,128)(2,1)S(1)}, bf16[1,176,1024]{2,1,0:T(8,128)(2,1)}, u32[]{:S(2)}) copy-start(bf16[1,176,1024]{2,1,0:T(8,128)(2,1)} %param.18) | copy-start | bytes 1081348
  7.2 92.5 %reduce-scatter.7.cloned.1.call-start = ((), (), s32[]{:S(2)}) async-start(), calls=%async_computation.6 | async-start | bytes 6127616
  11.7 0.7 copy-start.6
  11.7 88.1 %copy-start.4 = (bf16[88,1024]{1,0:T(8,128)(2,1)S(1)}, bf16[88,1024]{1,0:T(8,128)(2,1)}, u32[]{:S(2)}) copy-start(bf16[88,1024]{1,0:T(8,128)(2,1)} %param.10) | copy-start | bytes 540676
  11.7 89.2 %copy-start.7 = (f32[1024]{0:T(1024)S(1)}, f32[1024]{0:T(1024)}, u32[]{:S(2)}) copy-start(f32[1024]{0:T(1024)} %param.13) | copy-start | bytes 12292
  11.7 379.4 %reduce-scatter.5.cloned.1.call-start = ((), (), s32[]{:S(2)}) async-start(), calls=%async_computation.5 | async-start | bytes 12255232 | tf_op jit(solution)/shard_map/reduce_scatter | solution.py:84
  140.1 139.4 %copy-start.3 = (bf16[1,176,1024]{2,1,0:T(8,128)(2,1)S(1)}, bf16[1,176,1024]{2,1,0:T(8,128)(2,1)}, u32[]{:S(2)}) copy-start(bf16[1,176,1024]{2,1,0:T(8,128)(2,1)} %param.16) | copy-start | bytes 1081348
  275.2 4.2 copy-start.1
  279.4 5.9 %copy-start.9 = (bf16[1,176,1024]{2,1,0:T(8,128)(2,1)S(1)}, bf16[1,176,1024]{2,1,0:T(8,128)(2,1)}, u32[]{:S(2)}) copy-start(bf16[1,176,1024]{2,1,0:T(8,128)(2,1)} %param.17) | copy-start | bytes 1081348
  298.5 103.5 %copy-start.5 = (f32[1024,16]{0,1:T(8,128)S(1)}, f32[1024,16]{0,1:T(8,128)}, u32[]{:S(2)}) copy-start(f32[1024,16]{0,1:T(8,128)} %param.14) | copy-start | bytes 196612
  393.2 31.1 %all-to-all-start.2 = ((bf16[16,22,1024]{2,1,0:T(8,128)(2,1)}), bf16[16,22,1024]{2,1,0:T(8,128)(2,1)S(1)}, u32[]{:S(2)}, u32[]{:S(2)}) async-start(bf16[16,22,1024]{2,1,0:T(8,128)(2,1)} %reshape.117), calls=%async_computation.3 | async-start | bytes 1572864 | tf_op jit(solution)/shard_map/all_to_all | solution.py:91
  402.3 22.7 %copy-start.8 = (f32[1024]{0:T(1024)S(1)}, f32[1024]{0:T(1024)}, u32[]{:S(2)}) copy-start(f32[1024]{0:T(1024)} %param.19) | copy-start | bytes 12292
  425.0 0.8 copy-start.2
Sparse Core Ops, SparseCore 0:
  11.8 87.8 reduce-scatter.6
  298.7 92.3 reduce-scatter.4
